TPU v7x, 512 devices: a whole 4x4x16 slice. The times are simulated.
512 devices in a mesh: seq: 128 (over z, x, core), fsdp: 4 (over y).
Axes of the slice: x: 4, y: 4, z: 16, core: 2. Of those that a mesh axis runs over, the one named last changes fastest.
Arguments:
- query_key: bfloat16 [131072, 3072], P(('seq', 'fsdp')), may hold values from -48 to 48
- values: bfloat16 [131072, 3072], P(('seq', 'fsdp')), may hold values from -6 to 6
- cluster_ids: int32 [24, 1024], replicated, may hold values from 0 to 127, as said below
Outputs:
- attended: bfloat16 [131072, 3072], P(('seq', 'fsdp'))
Inputs may be any that keep to these rules, and one draw needn't show every extreme that they name: `cluster_ids`: for every head and cluster at most 10 blocks name that cluster, and for every head some cluster is named by exactly 10 blocks. Among the (head, block) pairs of one group of 6 consecutive heads and one run of 8 blocks starting at a multiple of 8, no cluster is named more than 1 times, and some cluster exactly 1 times; the blocks of one such run name distinct clusters for each head.
All inputs are finite; a program needn't handle non-finite values.
Results may differ from a plain program's by a relative error of at most 0.0027.
Values may be sent and summed in bfloat16 or wider, within the bound.
No kernel may reach another device: no remote copies, remote signals or barrier semaphores. Data moves between devices by JAX's collectives and lax.ppermute only.
A program may use at most 64 MiB of HBM per device.

v0:
```python
import math
import jax
import jax.numpy as jnp
from jax import lax
from jax.sharding import PartitionSpec as P

BLK = 128
masked_score = -1e30


def by_index(source_table, row_index):
    return source_table[jnp.clip(row_index, 0, source_table.shape[0] - 1)]


def softmax_group(key_rows, positions, alive_rows, score_scale):
    scores = jnp.dot(key_rows, key_rows.T, preferred_element_type=jnp.float32) * score_scale
    allowed = alive_rows[None, :] & (positions[None, :] <= positions[:, None])
    scores = jnp.where(allowed, scores, masked_score)
    row_peak = jnp.max(scores, axis=1, keepdims=True)
    weights = jnp.where(allowed, jnp.exp(scores - row_peak), 0.0)
    row_total = jnp.where(alive_rows[:, None], jnp.sum(weights, axis=1, keepdims=True), 1.0)
    return (weights.astype(jnp.bfloat16), row_total)


def shards(query_key, values, cluster_ids):
    seq_count = lax.axis_size("seq")
    group_count = lax.axis_size("fsdp")
    seq_index = lax.axis_index("seq")
    group_index = lax.axis_index("fsdp")
    heads_all = cluster_ids.shape[0]
    group_heads = heads_all // group_count
    head_dim = query_key.shape[1] // heads_all
    tok_rows = query_key.shape[0]
    shard_blocks = group_count * tok_rows // BLK
    all_blocks = cluster_ids.shape[1]
    item_count = group_heads * shard_blocks
    slot_count = max(1, item_count // seq_count)
    capacity = shard_blocks + min(shard_blocks // 4, seq_count - shard_blocks)
    group_rows = capacity * BLK
    send_rows = seq_count * slot_count
    score_scale = 1.0 / math.sqrt(head_dim)
    own_blocks = tok_rows // BLK
    keys_local = lax.all_to_all(query_key, "fsdp", split_axis=1, concat_axis=0, tiled=True)
    value_chunks = values.reshape(tok_rows, group_count, group_heads * head_dim)
    value_chunks, keys_local = lax.optimization_barrier((value_chunks, keys_local))
    by_shift = [lax.dynamic_index_in_dim(value_chunks, group_index, 1, keepdims=False)]
    for shift in range(1, group_count):
        outgoing = lax.dynamic_index_in_dim(
            value_chunks, (group_index + shift) % group_count, 1, keepdims=False
        )
        by_shift.append(
            lax.ppermute(
                outgoing,
                "fsdp",
                [(peer, (peer + shift) % group_count) for peer in range(group_count)],
            )
        )
    source_order = (group_index - jnp.arange(group_count, dtype=jnp.int32)) % group_count
    values_local = jnp.stack(by_shift)[source_order].reshape(
        group_count * tok_rows, group_heads * head_dim
    )

    def into_items(block_data):
        shaped = block_data.reshape(shard_blocks, BLK, group_heads, head_dim)
        return jnp.transpose(shaped, (2, 0, 1, 3)).reshape(item_count, BLK, head_dim)

    key_items = into_items(keys_local)
    value_items = into_items(values_local)
    group_ids = lax.dynamic_slice_in_dim(cluster_ids, group_index * group_heads, group_heads, 0)
    by_source = jnp.transpose(
        group_ids.reshape(group_heads, seq_count, shard_blocks), (1, 0, 2)
    ).reshape(seq_count, item_count)
    own_dest = lax.dynamic_index_in_dim(by_source, seq_index, 0, keepdims=False)
    item_ids = jnp.arange(item_count, dtype=jnp.int32)
    earlier = (own_dest[None, :] == own_dest[:, None]) & (item_ids[None, :] < item_ids[:, None])
    own_pos = own_dest * slot_count + jnp.sum(earlier.astype(jnp.int32), axis=1)
    row_ids = jnp.arange(send_rows, dtype=jnp.int32)
    slot_match = own_pos[None, :] == row_ids[:, None]
    send_pick = jnp.sum(jnp.where(slot_match, item_ids[None, :], 0), axis=1) + item_count * (
        1 - jnp.any(slot_match, axis=1).astype(jnp.int32)
    )
    key_send, group_ids = lax.optimization_barrier((by_index(key_items, send_pick), group_ids))
    arrived_k = lax.all_to_all(key_send, "seq", split_axis=0, concat_axis=0, tiled=True)
    value_send = by_index(value_items, send_pick)
    arrived_k, value_send = lax.optimization_barrier((arrived_k, value_send))
    arrived_v = lax.all_to_all(value_send, "seq", split_axis=0, concat_axis=0, tiled=True)
    by_source = jnp.transpose(
        group_ids.reshape(group_heads, seq_count, shard_blocks), (1, 0, 2)
    ).reshape(seq_count, item_count)
    received_mask = (by_source == seq_index).astype(jnp.int32)
    recv_pos = (
        jnp.arange(seq_count, dtype=jnp.int32)[:, None] * slot_count
        + jnp.cumsum(received_mask, axis=1)
        - received_mask
    )
    recv_by_head = jnp.transpose(
        recv_pos.reshape(seq_count, group_heads, shard_blocks), (1, 0, 2)
    ).reshape(group_heads * all_blocks)
    owned_mask = (group_ids == seq_index).astype(jnp.int32)
    ordinal = jnp.cumsum(owned_mask, axis=1) - owned_mask
    target = jnp.where(
        owned_mask > 0, jnp.arange(group_heads, dtype=jnp.int32)[:, None] * capacity + ordinal, -1
    ).reshape(group_heads * all_blocks)
    slot_ids = jnp.arange(group_heads * capacity, dtype=jnp.int32)
    matches = target[None, :] == slot_ids[:, None]
    present = jnp.any(matches, axis=1)
    source_row = jnp.sum(jnp.where(matches, recv_by_head[None, :], 0), axis=1) + send_rows * (
        1 - present.astype(jnp.int32)
    )
    block_ids = jnp.tile(jnp.arange(all_blocks, dtype=jnp.int32), group_heads)
    block_of = jnp.sum(jnp.where(matches, block_ids[None, :], 0), axis=1)
    key_grouped = by_index(arrived_k, source_row)
    value_grouped = by_index(arrived_v, source_row)
    positions = (block_of[:, None] * BLK + jnp.arange(BLK, dtype=jnp.int32)[None, :]).reshape(
        group_heads, group_rows
    )
    alive_rows = jnp.repeat(present, BLK).reshape(group_heads, group_rows)

    def one_head(operands):
        key_rows, where_at, alive_here = operands
        return softmax_group(key_rows, where_at, alive_here, score_scale)

    weights, totals = lax.map(
        one_head, (key_grouped.reshape(group_heads, group_rows, head_dim), positions, alive_rows)
    )
    value_rows = value_grouped.reshape(group_heads, group_rows, head_dim)
    back_match = source_row[None, :] == row_ids[:, None]
    back_pick = jnp.sum(
        jnp.where(back_match, slot_ids[None, :], 0), axis=1
    ) + group_heads * capacity * (1 - jnp.any(back_match, axis=1).astype(jnp.int32))
    weighted = jnp.einsum("hqk,hkd->hqd", weights, value_rows, preferred_element_type=jnp.float32)
    outputs = (
        (weighted / totals).astype(jnp.bfloat16).reshape(group_heads * capacity, BLK, head_dim)
    )
    returned = lax.all_to_all(
        by_index(outputs, back_pick), "seq", split_axis=0, concat_axis=0, tiled=True
    )
    own_output = by_index(returned, own_pos).reshape(
        group_heads, group_count, own_blocks, BLK, head_dim
    )
    gathered = lax.all_to_all(
        jnp.swapaxes(own_output, 0, 1), "fsdp", split_axis=0, concat_axis=0, tiled=True
    )
    token_major = jnp.transpose(gathered, (2, 3, 0, 1, 4))
    return token_major.reshape(tok_rows, heads_all * head_dim)


def solution(mesh):
    placed = (P(("seq", "fsdp"), None), P(("seq", "fsdp"), None), P())
    return jax.shard_map(
        shards, mesh=mesh, in_specs=placed, out_specs=P(("seq", "fsdp"), None), check_vma=False
    )
```

profile of v0, /device:TPU:70, one launch (start us, length us, event | category | flops | bytes accessed | tf_op | source)
XLA Modules:
  0.0 684.2 jit_solution(3121798839654760957)
XLA Ops:
  0.0 2.6 copy.60
  2.6 4.6 all-to-all-start
  7.2 1.0 reshape.313
  8.2 1.1 copy.64
  9.3 0.2 dynamic-slice_reduce_fusion.2
  9.5 0.2 convert_reduce_fusion
  9.8 1.6 copy.59
  11.8 16.1 %all-to-all-done = bf16[256,4,768]{0,2,1:T(8,128)(2,1)S(1)} async-done(((bf16[256,4,768]{0,2,1:T(8,128)(2,1)}), bf16[256,4,768]{0,2,1:T(8,128)(2,1)S(1)}, u32[]{:S(2)}, u32[]{:S(2)}) %all-to-all-start) | async-done | bytes 1572896 | tf_op jit(solution)/shard_map/all_to_all | solution.py:43
  27.9 0.7 copy.61
  28.6 0.8 copy.62
  29.4 0.4 copy.86
  29.8 1.1 copy.63
  31.0 3.1 gather_fusion
  34.1 18.9 %all-to-all-start.1 = ((bf16[128,128,128]{2,1,0:T(8,128)(2,1)}), bf16[128,128,128]{2,1,0:T(8,128)(2,1)}, u32[]{:S(2)}, u32[]{:S(2)}) async-start(bf16[128,128,128]{2,1,0:T(8,128)(2,1)} %gather_fusion), calls=%async_computation.1 | async-start | bytes 8388608 | tf_op jit(solution)/shard_map/all_to_all | solution.py:83
  53.3 1.7 reduce-window.6
  55.0 0.2 slice_reduce_fusion
  55.5 0.2 reshape.334
  56.2 0.2 broadcast_in_dim.121
  56.7 2.5 collective-permute-start
  59.4 4.0 collective-permute-start.1
  63.5 2.5 collective-permute-start.2
  66.3 0.6 select_reduce_fusion
  67.0 0.3 fusion.9
  67.9 11.5 %collective-permute-done = bf16[256,768]{1,0:T(8,128)(2,1)S(1)} collective-permute-done((bf16[256,768]{1,0:T(8,128)(2,1)S(1)}, bf16[256,768]{1,0:T(8,128)(2,1)S(1)}, u32[]{:S(2)}, u32[]{:S(2)}) %collective-permute-start) | collective-permute-done | bytes 393248 | tf_op jit(solution)/shard_map/ppermute | solution.py:52
  79.4 2.7 collective-permute-done.2
  82.1 0.7 copy-done.4
  82.9 1.2 pad_maximum_fusion
  84.0 0.6 gather_fusion.1
  84.7 1.0 copy.72
  85.8 0.6 reshape_reshape.4
  86.4 1.1 copy.73
  87.5 3.1 gather_fusion.2
  90.7 150.5 %all-to-all-done.1 = bf16[128,128,128]{2,1,0:T(8,128)(2,1)} async-done(((bf16[128,128,128]{2,1,0:T(8,128)(2,1)}), bf16[128,128,128]{2,1,0:T(8,128)(2,1)}, u32[]{:S(2)}, u32[]{:S(2)}) %all-to-all-start.1) | async-done | bytes 4194336 | tf_op jit(solution)/shard_map/all_to_all | solution.py:83
  241.2 8.9 %all-to-all-start.2 = ((bf16[128,128,128]{2,1,0:T(8,128)(2,1)}), bf16[128,128,128]{2,1,0:T(8,128)(2,1)}, u32[]{:S(2)}, u32[]{:S(2)}) async-start(bf16[128,128,128]{2,1,0:T(8,128)(2,1)} %gather_fusion.2), calls=%async_computation.2 | async-start | bytes 8388608 | tf_op jit(solution)/shard_map/all_to_all | solution.py:86
  250.2 3.1 gather_fusion.3
  253.3 46.0 %while.12 = (s32[]{:T(128)}, bf16[6,1280,1280]{1,2,0:T(8,128)(2,1)}, f32[6,1280,1]{1,0,2:T(8,128)S(1)}, pred[6,1280]{1,0:T(8,128)(4,1)S(1)}, s32[6,1280]{1,0:T(8...) while((s32[]{:T(128)}, bf16[6,1280,1280]{1,2,0:T(8,128)(2,1)}, ...), condition=%wide.region_12.13_spmd, body=%wide.region_9.12_spmd.sunk | while | flops 444005120 | bytes 23367272 | solution.py:123
  253.4 1.7 fusion.30
  255.1 3.4 fusion.31
  258.5 2.3 fusion.32
  261.0 1.7 fusion.30
  262.7 3.4 fusion.31
  266.1 2.3 fusion.32
  268.7 1.7 fusion.30
  270.4 3.4 fusion.31
  273.9 2.3 fusion.32
  276.4 1.7 fusion.30
  278.1 3.4 fusion.31
  281.5 2.3 fusion.32
  284.1 1.7 fusion.30
  285.8 3.4 fusion.31
  289.2 2.3 fusion.32
  291.7 1.7 fusion.30
  293.5 3.4 fusion.31
  296.8 2.3 fusion.32
  299.3 138.9 %all-to-all-done.2 = bf16[128,128,128]{2,1,0:T(8,128)(2,1)} async-done(((bf16[128,128,128]{2,1,0:T(8,128)(2,1)}), bf16[128,128,128]{2,1,0:T(8,128)(2,1)}, u32[]{:S(2)}, u32[]{:S(2)}) %all-to-all-start.2) | async-done | bytes 4194336 | tf_op jit(solution)/shard_map/all_to_all | solution.py:86
  438.2 4.4 gather_fusion.4
  442.6 11.0 %divide_convert_fusion = bf16[6,1280,128]{2,1,0:T(8,128)(2,1)S(1)} fusion(bf16[6,1280,1280]{1,2,0:T(8,128)(2,1)} %get-tuple-element.49, bf16[6,1280,128]{2,1,0:T(8,128)(2,1)} %bitcast.118, f32[6,1280]{1,0:T(8,128)S(1)} %bitcast.134), kind=kOutput, calls=%fused_computation.22 | convolution fusion | flops 2518548480 | bytes 23623680 | tf_op jit(solution)/shard_map/hqk,hkd->hqd/dot_general | solution.py:131
  453.6 3.1 gather_fusion.5
  456.6 8.9 %all-to-all-start.3 = ((bf16[128,128,128]{2,1,0:T(8,128)(2,1)}), bf16[128,128,128]{2,1,0:T(8,128)(2,1)}, u32[]{:S(2)}, u32[]{:S(2)}) async-start(bf16[128,128,128]{2,1,0:T(8,128)(2,1)} %gather_fusion.5), calls=%async_computation.3 | async-start | bytes 8388608 | tf_op jit(solution)/shard_map/all_to_all | solution.py:135
  465.6 188.1 %all-to-all-done.3 = bf16[128,128,128]{2,1,0:T(8,128)(2,1)} async-done(((bf16[128,128,128]{2,1,0:T(8,128)(2,1)}), bf16[128,128,128]{2,1,0:T(8,128)(2,1)}, u32[]{:S(2)}, u32[]{:S(2)}) %all-to-all-start.3) | async-done | bytes 4194336 | tf_op jit(solution)/shard_map/all_to_all | solution.py:135
  653.7 3.0 gather_fusion.6
  656.9 23.6 %all_to_all.39 = bf16[4,6,2,128,128]{4,3,2,1,0:T(8,128)(2,1)S(1)} all-to-all(bf16[4,6,2,128,128]{4,3,2,1,0:T(8,128)(2,1)S(1)} %copy.77), channel_id=1, replica_groups=mesh['seq'=128,'fsdp'=4] {'fsdp'}, dimensions={0} | all-to-all | bytes 3145728 | tf_op jit(solution)/shard_map/all_to_all | solution.py:141
  680.5 1.1 copy.81
  681.6 2.6 reshape.391
  (81 shorter events, 4.3 us)
Async XLA Ops:
  0.0 7.2 %copy-start = (s32[24,1024]{1,0:T(8,128)S(1)}, s32[24,1024]{1,0:T(8,128)}, u32[]{:S(2)}) copy-start(s32[24,1024]{1,0:T(8,128)} %param.7) | copy-start | bytes 294916
  2.6 7.2 %copy-start.3 = (bf16[256,3072]{1,0:T(8,128)(2,1)S(1)}, bf16[256,3072]{1,0:T(8,128)(2,1)}, u32[]{:S(2)}) copy-start(bf16[256,3072]{1,0:T(8,128)(2,1)} %param.6) | copy-start | bytes 4718596
  2.6 25.3 %all-to-all-start = ((bf16[256,4,768]{0,2,1:T(8,128)(2,1)}), bf16[256,4,768]{0,2,1:T(8,128)(2,1)S(1)}, u32[]{:S(2)}, u32[]{:S(2)}) async-start(bf16[256,4,768]{0,2,1:T(8,128)(2,1)} %bitcast.4), calls=%async_computation | async-start | bytes 3145728 | tf_op jit(solution)/shard_map/all_to_all | solution.py:43
  34.1 207.1 %all-to-all-start.1 = ((bf16[128,128,128]{2,1,0:T(8,128)(2,1)}), bf16[128,128,128]{2,1,0:T(8,128)(2,1)}, u32[]{:S(2)}, u32[]{:S(2)}) async-start(bf16[128,128,128]{2,1,0:T(8,128)(2,1)} %gather_fusion), calls=%async_computation.1 | async-start | bytes 8388608 | tf_op jit(solution)/shard_map/all_to_all | solution.py:83
  53.0 3.4 copy-start.2
  56.7 22.7 %collective-permute-start = (bf16[256,768]{1,0:T(8,128)(2,1)S(1)}, bf16[256,768]{1,0:T(8,128)(2,1)S(1)}, u32[]{:S(2)}, u32[]{:S(2)}) collective-permute-start(bf16[256,768]{1,0:T(8,128)(2,1)S(1)} %bitcast.124), channel_id=1, source_target_pairs={{0,1},{1,2},{2,3},{3,0},{4,5},{5,6},{6,7},{7,4},{8,9},{9,10},{10,1... | collective-permute-start | bytes 1179656 | tf_op jit(solution)/shard_map/ppermute | solution.py:52
  59.4 20.0 %collective-permute-start.1 = (bf16[256,768]{1,0:T(8,128)(2,1)S(1)}, bf16[256,768]{1,0:T(8,128)(2,1)S(1)}, u32[]{:S(2)}, u32[]{:S(2)}) collective-permute-start(bf16[256,768]{1,0:T(8,128)(2,1)S(1)} %bitcast.125), channel_id=1, source_target_pairs={{0,2},{1,3},{2,0},{3,1},{4,6},{5,7},{6,4},{7,5},{8,10},{9,11},{10,... | collective-permute-start | bytes 1179656 | tf_op jit(solution)/shard_map/ppermute | solution.py:52
  63.5 18.6 %collective-permute-start.2 = (bf16[256,768]{1,0:T(8,128)(2,1)S(1)}, bf16[256,768]{1,0:T(8,128)(2,1)S(1)}, u32[]{:S(2)}, u32[]{:S(2)}) collective-permute-start(bf16[256,768]{1,0:T(8,128)(2,1)S(1)} %bitcast.126), channel_id=1, source_target_pairs={{0,3},{1,0},{2,1},{3,2},{4,7},{5,4},{6,5},{7,6},{8,11},{9,8},{10,9... | collective-permute-start | bytes 1179656 | tf_op jit(solution)/shard_map/ppermute | solution.py:52
  82.1 0.7 copy-start.4
  241.2 197.1 %all-to-all-start.2 = ((bf16[128,128,128]{2,1,0:T(8,128)(2,1)}), bf16[128,128,128]{2,1,0:T(8,128)(2,1)}, u32[]{:S(2)}, u32[]{:S(2)}) async-start(bf16[128,128,128]{2,1,0:T(8,128)(2,1)} %gather_fusion.2), calls=%async_computation.2 | async-start | bytes 8388608 | tf_op jit(solution)/shard_map/all_to_all | solution.py:86
  456.6 197.1 %all-to-all-start.3 = ((bf16[128,128,128]{2,1,0:T(8,128)(2,1)}), bf16[128,128,128]{2,1,0:T(8,128)(2,1)}, u32[]{:S(2)}, u32[]{:S(2)}) async-start(bf16[128,128,128]{2,1,0:T(8,128)(2,1)} %gather_fusion.5), calls=%async_computation.3 | async-start | bytes 8388608 | tf_op jit(solution)/shard_map/all_to_all | solution.py:135
  680.5 3.7 copy-start.1
where the time goes:
time: 685 us; the launch traced here: 684 us
  waiting for transfers between devices  508 us (74%)
  starting transfers between devices  50.4 us (7%)
  local copies, waits for them, and re-layouts  40.9 us (6%)
  other arithmetic  39.3 us (6%)
  blocking collectives  23.6 us (3%)
  matrix products  21.4 us (3%)
    all_to_all x1, waiting for transfers between devices, shards(): lax.all_to_all(by_index(outputs, back_pick), 'seq', split_axis=0, concat_...  188 us
    all_to_all x1, waiting for transfers between devices, shards(): lax.all_to_all(key_send, 'seq', split_axis=0, concat_axis=0, tiled=True)  151 us
    all_to_all x1, waiting for transfers between devices, shards(): lax.all_to_all(value_send, 'seq', split_axis=0, concat_axis=0, tiled=True)  139 us
    all_to_all x1, blocking collectives, shards(): lax.all_to_all(jnp.swapaxes(own_output, 0, 1), 'fsdp', split_axis=0, conc...  23.6 us
    dynamic_update_slice x12, other arithmetic, shards(): lax.map(one_head, (key_grouped.reshape(group_heads, group_rows, head_dim)...  20.4 us
    gather x6, local copies, waits for them, and re-layouts, by_index(): return source_table[jnp.clip(row_index, 0, source_table.shape[0] - 1)]  19.8 us
    all_to_all x1, starting transfers between devices, shards(): lax.all_to_all(key_send, 'seq', split_axis=0, concat_axis=0, tiled=True)  18.9 us
    all_to_all x1, waiting for transfers between devices, shards(): lax.all_to_all(query_key, 'fsdp', split_axis=1, concat_axis=0, tiled=True)  16.1 us
  transfers between devices with their start and end apart: 7, of which 6 were waited for; matrix products, arithmetic and copies ran while one was open for 10% of the time, Pallas kernels for 0%

commit v1 on v0

--- a/solution.py
+++ b/solution.py
@@ -6,6 +6,22 @@
 
 BLK = 128
 masked_score = -1e30
+
+
+def pairwise_exchange(shard, axis, split, join):
+    ways, here = (lax.axis_size(axis), lax.axis_index(axis))
+    width = shard.shape[split] // ways
+    dims = list(shard.shape)
+    dims[split] = width
+    height = dims[join]
+    dims[join] = height * ways
+    full = jnp.zeros(dims, shard.dtype)
+    for mask in range(ways):
+        part = lax.dynamic_slice_in_dim(shard, (here ^ mask) * width, width, axis=split)
+        if mask:
+            part = lax.ppermute(part, axis, [(d, d ^ mask) for d in range(ways)])
+        full = lax.dynamic_update_slice_in_dim(full, part, (here ^ mask) * height, axis=join)
+    return full
 
 
 def by_index(source_table, row_index):
@@ -138,9 +154,7 @@
     own_output = by_index(returned, own_pos).reshape(
         group_heads, group_count, own_blocks, BLK, head_dim
     )
-    gathered = lax.all_to_all(
-        jnp.swapaxes(own_output, 0, 1), "fsdp", split_axis=0, concat_axis=0, tiled=True
-    )
+    gathered = pairwise_exchange(jnp.swapaxes(own_output, 0, 1), "fsdp", 0, 0)
     token_major = jnp.transpose(gathered, (2, 3, 0, 1, 4))
     return token_major.reshape(tok_rows, heads_all * head_dim)
 

time: 685 us -> 690 us (level)
  blocking collectives: 23.6 us -> 0 us
  waiting for transfers between devices: 508 us -> 523 us
  starting transfers between devices: 50.4 us -> 60.8 us
    all_to_all x1 -> x0, blocking collectives: 23.6 us -> none  [shards(): lax.all_to_all(jnp.swapaxes(own_output, 0, 1), 'fsdp', split_axis=0, conc...]
    ppermute x0 -> x3, waiting for transfers between devices: none -> 15.5 us  [pairwise_exchange(): part = lax.ppermute(part, axis, [(d, d ^ mask) for d in range(ways)])]
    ppermute x0 -> x3, starting transfers between devices: none -> 10.4 us  [pairwise_exchange(): part = lax.ppermute(part, axis, [(d, d ^ mask) for d in range(ways)])]
  transfers between devices with their start and end apart: 7 -> 10, of which waited for: 6 -> 9; matrix products, arithmetic and copies ran while one was open for 10% -> 10% of each run, Pallas kernels for 0% -> 0%
where the time goes in v1:
time: 690 us; the launch traced here: 689 us
  waiting for transfers between devices  523 us (76%)
  starting transfers between devices  60.8 us (9%)
  local copies, waits for them, and re-layouts  43.4 us (6%)
  other arithmetic  39.3 us (6%)
  matrix products  21.4 us (3%)
    all_to_all x1, waiting for transfers between devices, shards(): lax.all_to_all(by_index(outputs, back_pick), 'seq', split_axis=0, concat_...  188 us
    all_to_all x1, waiting for transfers between devices, shards(): lax.all_to_all(key_send, 'seq', split_axis=0, concat_axis=0, tiled=True)  151 us
    all_to_all x1, waiting for transfers between devices, shards(): lax.all_to_all(value_send, 'seq', split_axis=0, concat_axis=0, tiled=True)  139 us
    dynamic_update_slice x12, other arithmetic, shards(): lax.map(one_head, (key_grouped.reshape(group_heads, group_rows, head_dim)...  20.4 us
    gather x6, local copies, waits for them, and re-layouts, by_index(): return source_table[jnp.clip(row_index, 0, source_table.shape[0] - 1)]  19.8 us
    all_to_all x1, starting transfers between devices, shards(): lax.all_to_all(key_send, 'seq', split_axis=0, concat_axis=0, tiled=True)  18.9 us
    all_to_all x1, waiting for transfers between devices, shards(): lax.all_to_all(query_key, 'fsdp', split_axis=1, concat_axis=0, tiled=True)  16.1 us
    ppermute x3, waiting for transfers between devices, pairwise_exchange(): part = lax.ppermute(part, axis, [(d, d ^ mask) for d in range(ways)])  15.5 us
  transfers between devices with their start and end apart: 10, of which 9 were waited for; matrix products, arithmetic and copies ran while one was open for 10% of the time, Pallas kernels for 0%

profile of v1, /device:TPU:70, one launch (start us, length us, event | category | flops | bytes accessed | tf_op | source)
XLA Modules:
  0.0 689.1 jit_solution(1056705197599896577)
XLA Ops:
  0.0 2.6 copy.49
  2.6 4.6 all-to-all-start
  7.2 1.0 reshape.317
  8.2 1.1 copy.53
  9.8 1.6 copy.48
  11.8 16.1 %all-to-all-done = bf16[256,4,768]{0,2,1:T(8,128)(2,1)S(1)} async-done(((bf16[256,4,768]{0,2,1:T(8,128)(2,1)}), bf16[256,4,768]{0,2,1:T(8,128)(2,1)S(1)}, u32[]{:S(2)}, u32[]{:S(2)}) %all-to-all-start) | async-done | bytes 1572896 | tf_op jit(solution)/shard_map/all_to_all | solution.py:59
  27.9 0.7 copy.50
  28.6 0.8 copy.51
  29.4 0.4 copy.79
  29.8 1.1 copy.52
  31.0 3.1 gather_fusion
  34.1 18.9 %all-to-all-start.1 = ((bf16[128,128,128]{2,1,0:T(8,128)(2,1)}), bf16[128,128,128]{2,1,0:T(8,128)(2,1)}, u32[]{:S(2)}, u32[]{:S(2)}) async-start(bf16[128,128,128]{2,1,0:T(8,128)(2,1)} %gather_fusion), calls=%async_computation.1 | async-start | bytes 8388608 | tf_op jit(solution)/shard_map/all_to_all | solution.py:99
  53.3 1.7 reduce-window.6
  56.7 2.5 collective-permute-start
  59.4 4.0 collective-permute-start.1
  63.5 2.5 collective-permute-start.2
  66.3 0.6 select_reduce_fusion
  67.9 11.5 %collective-permute-done = bf16[256,768]{1,0:T(8,128)(2,1)S(1)} collective-permute-done((bf16[256,768]{1,0:T(8,128)(2,1)S(1)}, bf16[256,768]{1,0:T(8,128)(2,1)S(1)}, u32[]{:S(2)}, u32[]{:S(2)}) %collective-permute-start) | collective-permute-done | bytes 393248 | tf_op jit(solution)/shard_map/ppermute | solution.py:68
  79.4 2.7 collective-permute-done.2
  82.1 0.7 copy-done.4
  82.9 1.2 pad_maximum_fusion
  84.0 0.6 gather_fusion.1
  84.7 1.0 copy.61
  85.8 0.6 reshape_reshape.4
  86.4 1.1 copy.62
  87.5 3.1 gather_fusion.2
  90.7 150.5 %all-to-all-done.1 = bf16[128,128,128]{2,1,0:T(8,128)(2,1)} async-done(((bf16[128,128,128]{2,1,0:T(8,128)(2,1)}), bf16[128,128,128]{2,1,0:T(8,128)(2,1)}, u32[]{:S(2)}, u32[]{:S(2)}) %all-to-all-start.1) | async-done | bytes 4194336 | tf_op jit(solution)/shard_map/all_to_all | solution.py:99
  241.2 8.9 %all-to-all-start.2 = ((bf16[128,128,128]{2,1,0:T(8,128)(2,1)}), bf16[128,128,128]{2,1,0:T(8,128)(2,1)}, u32[]{:S(2)}, u32[]{:S(2)}) async-start(bf16[128,128,128]{2,1,0:T(8,128)(2,1)} %gather_fusion.2), calls=%async_computation.2 | async-start | bytes 8388608 | tf_op jit(solution)/shard_map/all_to_all | solution.py:102
  250.2 3.1 gather_fusion.3
  253.3 46.0 %while.12 = (s32[]{:T(128)}, bf16[6,1280,1280]{1,2,0:T(8,128)(2,1)}, f32[6,1280,1]{1,0,2:T(8,128)S(1)}, pred[6,1280]{1,0:T(8,128)(4,1)S(1)}, s32[6,1280]{1,0:T(8...) while((s32[]{:T(128)}, bf16[6,1280,1280]{1,2,0:T(8,128)(2,1)}, ...), condition=%wide.region_12.13_spmd, body=%wide.region_9.12_spmd.sunk | while | flops 444005120 | bytes 23367272 | solution.py:139
  253.4 1.7 fusion.30
  255.1 3.4 fusion.31
  258.5 2.3 fusion.32
  261.0 1.7 fusion.30
  262.7 3.4 fusion.31
  266.1 2.3 fusion.32
  268.7 1.7 fusion.30
  270.4 3.4 fusion.31
  273.9 2.3 fusion.32
  276.4 1.7 fusion.30
  278.1 3.4 fusion.31
  281.5 2.3 fusion.32
  284.1 1.7 fusion.30
  285.8 3.4 fusion.31
  289.2 2.3 fusion.32
  291.7 1.7 fusion.30
  293.5 3.4 fusion.31
  296.8 2.3 fusion.32
  299.3 138.9 %all-to-all-done.2 = bf16[128,128,128]{2,1,0:T(8,128)(2,1)} async-done(((bf16[128,128,128]{2,1,0:T(8,128)(2,1)}), bf16[128,128,128]{2,1,0:T(8,128)(2,1)}, u32[]{:S(2)}, u32[]{:S(2)}) %all-to-all-start.2) | async-done | bytes 4194336 | tf_op jit(solution)/shard_map/all_to_all | solution.py:102
  438.2 4.4 gather_fusion.4
  442.6 11.0 %divide_convert_fusion = bf16[6,1280,128]{2,1,0:T(8,128)(2,1)S(1)} fusion(bf16[6,1280,1280]{1,2,0:T(8,128)(2,1)} %get-tuple-element.49, bf16[6,1280,128]{2,1,0:T(8,128)(2,1)} %bitcast.129, f32[6,1280]{1,0:T(8,128)S(1)} %bitcast.148), kind=kOutput, calls=%fused_computation.22 | convolution fusion | flops 2518548480 | bytes 23623680 | tf_op jit(solution)/shard_map/hqk,hkd->hqd/dot_general | solution.py:147
  453.6 3.1 gather_fusion.5
  456.6 9.0 %all-to-all-start.3 = ((bf16[128,128,128]{2,1,0:T(8,128)(2,1)}), bf16[128,128,128]{2,1,0:T(8,128)(2,1)}, u32[]{:S(2)}, u32[]{:S(2)}) async-start(bf16[128,128,128]{2,1,0:T(8,128)(2,1)} %gather_fusion.5), calls=%async_computation.3 | async-start | bytes 8388608 | tf_op jit(solution)/shard_map/all_to_all | solution.py:151
  465.6 188.1 %all-to-all-done.3 = bf16[128,128,128]{2,1,0:T(8,128)(2,1)} async-done(((bf16[128,128,128]{2,1,0:T(8,128)(2,1)}), bf16[128,128,128]{2,1,0:T(8,128)(2,1)}, u32[]{:S(2)}, u32[]{:S(2)}) %all-to-all-start.3) | async-done | bytes 4194336 | tf_op jit(solution)/shard_map/all_to_all | solution.py:151
  653.7 3.0 gather_fusion.6
  656.9 0.4 copy.74
  657.3 2.5 collective-permute-start.3
  660.2 4.0 collective-permute-start.4
  665.1 4.0 collective-permute-start.5
  669.0 1.3 broadcast_in_dim.113
  670.7 0.5 collective-permute-done.3
  671.5 7.8 %collective-permute-done.4 = bf16[1,6,2,128,128]{3,2,4,1,0:T(2,128)(2,1)S(1)} collective-permute-done((bf16[1,6,2,128,128]{3,2,4,1,0:T(2,128)(2,1)S(1)}, bf16[1,6,2,128,128]{3,2,4,1,0:T(2,128)(2,1)S(1)}, u32[]{:S(2)}, u32[]{:S(2)}) %collective-permute-start.4) | collective-permute-done | bytes 393248 | tf_op jit(solution)/shard_map/ppermute | solution.py:22
  679.7 7.2 %collective-permute-done.5 = bf16[1,6,2,128,128]{3,2,4,1,0:T(2,128)(2,1)S(1)} collective-permute-done((bf16[1,6,2,128,128]{3,2,4,1,0:T(2,128)(2,1)S(1)}, bf16[1,6,2,128,128]{3,2,4,1,0:T(2,128)(2,1)S(1)}, u32[]{:S(2)}, u32[]{:S(2)}) %collective-permute-start.5) | collective-permute-done | bytes 393248 | tf_op jit(solution)/shard_map/ppermute | solution.py:22
  687.4 1.7 copy.70
  (95 shorter events, 8.3 us)
Async XLA Ops:
  0.0 7.2 %copy-start = (s32[24,1024]{1,0:T(8,128)S(1)}, s32[24,1024]{1,0:T(8,128)}, u32[]{:S(2)}) copy-start(s32[24,1024]{1,0:T(8,128)} %param.7) | copy-start | bytes 294916
  2.6 7.2 %copy-start.3 = (bf16[256,3072]{1,0:T(8,128)(2,1)S(1)}, bf16[256,3072]{1,0:T(8,128)(2,1)}, u32[]{:S(2)}) copy-start(bf16[256,3072]{1,0:T(8,128)(2,1)} %param.6) | copy-start | bytes 4718596
  2.6 25.3 %all-to-all-start = ((bf16[256,4,768]{0,2,1:T(8,128)(2,1)}), bf16[256,4,768]{0,2,1:T(8,128)(2,1)S(1)}, u32[]{:S(2)}, u32[]{:S(2)}) async-start(bf16[256,4,768]{0,2,1:T(8,128)(2,1)} %bitcast.4), calls=%async_computation | async-start | bytes 3145728 | tf_op jit(solution)/shard_map/all_to_all | solution.py:59
  34.1 207.1 %all-to-all-start.1 = ((bf16[128,128,128]{2,1,0:T(8,128)(2,1)}), bf16[128,128,128]{2,1,0:T(8,128)(2,1)}, u32[]{:S(2)}, u32[]{:S(2)}) async-start(bf16[128,128,128]{2,1,0:T(8,128)(2,1)} %gather_fusion), calls=%async_computation.1 | async-start | bytes 8388608 | tf_op jit(solution)/shard_map/all_to_all | solution.py:99
  53.0 3.4 copy-start.2
  56.7 22.7 %collective-permute-start = (bf16[256,768]{1,0:T(8,128)(2,1)S(1)}, bf16[256,768]{1,0:T(8,128)(2,1)S(1)}, u32[]{:S(2)}, u32[]{:S(2)}) collective-permute-start(bf16[256,768]{1,0:T(8,128)(2,1)S(1)} %bitcast.135), channel_id=1, source_target_pairs={{0,1},{1,2},{2,3},{3,0},{4,5},{5,6},{6,7},{7,4},{8,9},{9,10},{10,1... | collective-permute-start | bytes 1179656 | tf_op jit(solution)/shard_map/ppermute | solution.py:68
  59.4 20.0 %collective-permute-start.1 = (bf16[256,768]{1,0:T(8,128)(2,1)S(1)}, bf16[256,768]{1,0:T(8,128)(2,1)S(1)}, u32[]{:S(2)}, u32[]{:S(2)}) collective-permute-start(bf16[256,768]{1,0:T(8,128)(2,1)S(1)} %bitcast.136), channel_id=1, source_target_pairs={{0,2},{1,3},{2,0},{3,1},{4,6},{5,7},{6,4},{7,5},{8,10},{9,11},{10,... | collective-permute-start | bytes 1179656 | tf_op jit(solution)/shard_map/ppermute | solution.py:68
  63.5 18.6 %collective-permute-start.2 = (bf16[256,768]{1,0:T(8,128)(2,1)S(1)}, bf16[256,768]{1,0:T(8,128)(2,1)S(1)}, u32[]{:S(2)}, u32[]{:S(2)}) collective-permute-start(bf16[256,768]{1,0:T(8,128)(2,1)S(1)} %bitcast.137), channel_id=1, source_target_pairs={{0,3},{1,0},{2,1},{3,2},{4,7},{5,4},{6,5},{7,6},{8,11},{9,8},{10,9... | collective-permute-start | bytes 1179656 | tf_op jit(solution)/shard_map/ppermute | solution.py:68
  82.1 0.7 copy-start.4
  241.2 197.1 %all-to-all-start.2 = ((bf16[128,128,128]{2,1,0:T(8,128)(2,1)}), bf16[128,128,128]{2,1,0:T(8,128)(2,1)}, u32[]{:S(2)}, u32[]{:S(2)}) async-start(bf16[128,128,128]{2,1,0:T(8,128)(2,1)} %gather_fusion.2), calls=%async_computation.2 | async-start | bytes 8388608 | tf_op jit(solution)/shard_map/all_to_all | solution.py:102
  456.6 197.1 %all-to-all-start.3 = ((bf16[128,128,128]{2,1,0:T(8,128)(2,1)}), bf16[128,128,128]{2,1,0:T(8,128)(2,1)}, u32[]{:S(2)}, u32[]{:S(2)}) async-start(bf16[128,128,128]{2,1,0:T(8,128)(2,1)} %gather_fusion.5), calls=%async_computation.3 | async-start | bytes 8388608 | tf_op jit(solution)/shard_map/all_to_all | solution.py:151
  657.3 13.9 %collective-permute-start.3 = (bf16[1,6,2,128,128]{3,2,4,1,0:T(2,128)(2,1)S(1)}, bf16[1,6,2,128,128]{3,2,4,1,0:T(2,128)(2,1)S(1)}, u32[]{:S(2)}, u32[]{:S(2)}) collective-permute-start(bf16[1,6,2,128,128]{3,2,4,1,0:T(2,128)(2,1)S(1)} %bitcast.140), channel_id=1, source_target_pairs={{0,1},{1,0},{2,3},{3,2},{4,5},{5,4},{6,7},{7,6},{8,9},{9,8},{10,11... | collective-permute-start | bytes 1179656 | tf_op jit(solution)/shard_map/ppermute | solution.py:22
  660.2 19.1 %collective-permute-start.4 = (bf16[1,6,2,128,128]{3,2,4,1,0:T(2,128)(2,1)S(1)}, bf16[1,6,2,128,128]{3,2,4,1,0:T(2,128)(2,1)S(1)}, u32[]{:S(2)}, u32[]{:S(2)}) collective-permute-start(bf16[1,6,2,128,128]{3,2,4,1,0:T(2,128)(2,1)S(1)} %bitcast.138), channel_id=1, source_target_pairs={{0,2},{1,3},{2,0},{3,1},{4,6},{5,7},{6,4},{7,5},{8,10},{9,11},{10,... | collective-permute-start | bytes 1179656 | tf_op jit(solution)/shard_map/ppermute | solution.py:22
  665.1 21.8 %collective-permute-start.5 = (bf16[1,6,2,128,128]{3,2,4,1,0:T(2,128)(2,1)S(1)}, bf16[1,6,2,128,128]{3,2,4,1,0:T(2,128)(2,1)S(1)}, u32[]{:S(2)}, u32[]{:S(2)}) collective-permute-start(bf16[1,6,2,128,128]{3,2,4,1,0:T(2,128)(2,1)S(1)} %bitcast.139), channel_id=1, source_target_pairs={{0,3},{1,2},{2,1},{3,0},{4,7},{5,6},{6,5},{7,4},{8,11},{9,10},{10,... | collective-permute-start | bytes 1179656 | tf_op jit(solution)/shard_map/ppermute | solution.py:22
  687.2 2.0 copy-start.1
